TPU v7x, 256 devices: a whole 4x4x8 slice. The times are simulated.
256 devices in a mesh: axial: 16 (over x_lo, y, core), azim: 16 (over z, x_hi).
Axes of the slice: x: 4 (x_hi: 2, x_lo: 2; x = x_hi * 2 + x_lo), y: 4, z: 8, core: 2. Of those that a mesh axis runs over, the one named last changes fastest.
Arguments:
- coil_density: float32 [512, 256, 128], P('azim', 'axial'), may hold values from -6 to 6
- coil_mask: int32 [512, 256, 128], P('azim', 'axial'), may hold values 0 or 1
- drive: float32 [2], replicated, may hold values from 0.5 to 2
- potential: float32 [512, 256, 128], P('azim', 'axial'), may hold values from -6 to 6
- tile_weight: float32 [512, 64, 64], P('azim'), may hold values from -0.75 to 0.75
- relay_owner: int32 [2, 512, 16], P(None, 'azim', 'axial'), may hold values from 0 to 2
- relay_slot: int32 [2, 512, 16], P(None, 'azim', 'axial'), may hold values from 0 to 31, as said below
- velocity: float32 [512, 256, 128], P('azim', 'axial'), may hold values from -3 to 3
- strain: float32 [512, 256, 128], P('azim', 'axial'), may hold values from -3 to 3
- plastic: float32 [512, 256, 128], P('azim', 'axial'), may hold values from -0.6 to 0.6
Outputs:
- field_out: float32 [512, 256, 128], P('azim', 'axial')
- velocity_out: float32 [512, 256, 128], P('azim', 'axial')
- strain_out: float32 [512, 256, 128], P('azim', 'axial')
- plastic_out: float32 [512, 256, 128], P('azim', 'axial')
Inputs may be any that keep to these rules, and one draw needn't show every extreme that they name: `relay_slot`: for each step and axial block, the values over the 32 azimuthal cells of one sector are a permutation of 0 to 31.
All inputs are finite; a program needn't handle non-finite values. No bound on the sum of `coil_mask` on one device may be relied on, other than what follows from the above.
Results may differ from a plain program's by a relative error of at most 0.00011.
Values sent between devices are 32-bit elements; how exact they have to be, the bound alone decides.
No kernel may reach another device: no remote copies, remote signals or barrier semaphores. Data moves between devices by JAX's collectives and lax.ppermute only.
A program may use at most 64 MiB of HBM per device.

v0:
```python
import math
import jax
import jax.numpy as jnp
from jax import lax
from jax.sharding import PartitionSpec as P

STEPS = 2
SWEEPS = 3
HIGH = lax.Precision.HIGHEST
KAPPA = 2.0
AIR_TERM = 0.05
R_CORE = 16.0
MU_COIL = 1.0
FORCE_K = 1.0
E_MOD = 1.0
YIELD_ZERO = 0.5
HARDEN = 0.3
TIME_STEP = 0.5
STIFFNESS = 0.5
DAMPING = 0.9


def with_halo(block, sides, width):
    for axis, dim in sides:
        count = lax.axis_size(axis)
        forward = [(i, i + 1) for i in range(count - 1)]
        backward = [(target, source) for source, target in forward]
        low = lax.ppermute(
            lax.slice_in_dim(block, block.shape[dim] - width, None, axis=dim), axis, forward
        )
        high = lax.ppermute(lax.slice_in_dim(block, 0, width, axis=dim), axis, backward)
        block = jnp.concatenate([low, block, high], axis=dim)
    return block


def shifted(array, axis, by):
    devices = lax.axis_size(axis)
    pairs = [(i, i + by) for i in range(devices) if 0 <= i + by < devices]
    return lax.ppermute(array, axis, pairs)


def harmonic_table(azimuth, harmonic, count_all):
    half_count = count_all // 2
    orders = jnp.where(harmonic <= half_count, harmonic, harmonic - half_count)
    phases = azimuth[:, None] * orders[None, :] % count_all
    angles = phases.astype(jnp.float32) * (2.0 * math.pi / count_all)
    return jnp.where(harmonic[None, :] <= half_count, jnp.cos(angles), jnp.sin(angles))


def harmonic_weight(harmonic, count_all):
    half_count = count_all // 2
    edge_mode = (harmonic == 0) | (harmonic == half_count)
    return jnp.where(edge_mode, 1.0 / count_all, 2.0 / count_all).astype(jnp.float32)


def harmonic_order(harmonic, count_all):
    half_count = count_all // 2
    return jnp.where(harmonic <= half_count, harmonic, harmonic - half_count).astype(jnp.float32)


def radial_profiles(radial_count, band_start, band_width):
    cell_index = jnp.arange(radial_count, dtype=jnp.int32)
    radius = R_CORE + cell_index.astype(jnp.float32)
    inside = (cell_index >= band_start) & (cell_index < band_start + band_width)
    conduct = jnp.where(inside, KAPPA, AIR_TERM).astype(jnp.float32)
    coil_zone = (cell_index < band_start).astype(jnp.float32)
    return (radius, conduct, coil_zone)


def radial_sum(iterate):
    radial_pad = jnp.pad(iterate, ((0, 0), (0, 0), (1, 1)))
    return radial_pad[:, :, 2:] + radial_pad[:, :, :-2]


def lorentz(padded, previous, conduct, radius, band_start, band_width):
    current_field = padded[:, 1:-1]
    axial_slope = (padded[:, 2:] - padded[:, :-2]) * 0.5
    radial_pad = jnp.pad(current_field, ((0, 0), (0, 0), (1, 1)))
    radial_slope = (radial_pad[:, :, 2:] - radial_pad[:, :, :-2]) * 0.5
    b_axial = radial_slope + current_field / radius
    eddy_current = -conduct * (current_field - previous)
    force_radial = FORCE_K * eddy_current * b_axial
    force_axial = FORCE_K * eddy_current * axial_slope
    return jnp.concatenate(
        [
            force_radial[..., band_start : band_start + band_width],
            force_axial[..., band_start : band_start + band_width],
        ],
        axis=-1,
    )


def plastic_update(load, velocity, strain, plastic):
    trial_stress = E_MOD * (strain - plastic)
    excess = jnp.abs(trial_stress) - YIELD_ZERO
    increment = (
        trial_stress
        * jnp.maximum(excess, 0.0)
        / ((E_MOD + HARDEN) * jnp.maximum(jnp.abs(trial_stress), YIELD_ZERO))
    )
    plastic = plastic + increment
    stress = E_MOD * (strain - plastic)
    velocity = DAMPING * velocity + TIME_STEP * (load - STIFFNESS * stress)
    strain = strain + TIME_STEP * velocity
    return (velocity, strain, plastic)


def transform(parts, table_rows, all_index):
    flat_shape = parts.shape
    columns_all = parts.reshape(flat_shape[0], -1)
    spread = lax.all_to_all(columns_all, "azim", split_axis=1, concat_axis=0, tiled=True)
    full_table = table_rows(all_index, all_index)
    mixed = jnp.dot(full_table.T, spread, precision=HIGH, preferred_element_type=jnp.float32)
    joined = lax.all_to_all(mixed, "azim", split_axis=0, concat_axis=1, tiled=True)
    return joined.reshape(flat_shape)


def shards(
    coil_density,
    coil_mask,
    drive,
    potential,
    tile_weight,
    relay_owner,
    relay_slot,
    velocity,
    strain,
    plastic,
):
    local_count = potential.shape[0]
    axial_cells = potential.shape[1]
    radial_cells = potential.shape[2]
    band_width = tile_weight.shape[1]
    azim_total = local_count * lax.axis_size("azim")
    own_index = lax.axis_index("azim") * local_count + jnp.arange(local_count, dtype=jnp.int32)
    all_index = jnp.arange(azim_total, dtype=jnp.int32)
    band_start = radial_cells // 4
    radius, conduct, coil_zone = radial_profiles(radial_cells, band_start, band_width)
    orders = harmonic_order(own_index, azim_total)
    diagonal_term = (
        4.0 + conduct[None, None, :] + (orders[:, None, None] / radius[None, None, :]) ** 2
    )

    def forward_rows(rows_in, rows_out):
        return harmonic_table(rows_in, rows_out, azim_total)

    def inverse_rows(rows_in, rows_out):
        return (
            harmonic_table(rows_out, rows_in, azim_total).T
            * harmonic_weight(rows_in, azim_total)[:, None]
        )

    slot_range = jnp.arange(local_count, dtype=jnp.int32)
    field = potential
    for step_index in range(STEPS):
        source = drive[step_index] * coil_density * coil_mask.astype(jnp.float32) * coil_zone
        stacked = jnp.stack([source, field], axis=1)
        modes = transform(stacked, forward_rows, all_index)
        right_side = MU_COIL * modes[:, 0] + conduct * modes[:, 1]
        iterate = modes[:, 1]
        for sweep_index in range(SWEEPS):
            axial_pad = with_halo(iterate, (("axial", 1),), 1)
            nearby = axial_pad[:, 2:] + axial_pad[:, :-2] + radial_sum(iterate)
            iterate = (right_side + nearby) / diagonal_term
        new_field = transform(iterate[:, None], inverse_rows, all_index)[:, 0]
        padded = with_halo(new_field, (("axial", 1),), 1)
        tiles = lorentz(padded, field, conduct, radius, band_start, band_width)
        slot_table = (relay_slot[step_index, :, 0][:, None] == slot_range[None, :]).astype(
            jnp.float32
        )
        owner_now = relay_owner[step_index, :, 0]

        def place(target):
            chosen = (owner_now == target).astype(jnp.float32)
            return jnp.einsum(
                "jcw,jp->pcw", tiles * chosen[:, None, None], slot_table, precision=HIGH
            )

        from_below = shifted(place(2), "axial", 1)
        from_above = shifted(place(0), "axial", -1)
        received = (place(1) + from_below + from_above).reshape(
            local_count, axial_cells, 2, band_width
        )
        load = jnp.einsum("aqr,azcr->azcq", tile_weight, received, precision=HIGH).reshape(
            local_count, axial_cells, 2 * band_width
        )
        velocity, strain, plastic = plastic_update(load, velocity, strain, plastic)
        field = new_field
    return (field, velocity, strain, plastic)


def solution(mesh):
    placed = (
        P("azim", "axial", None),
        P("azim", "axial", None),
        P(),
        P("azim", "axial", None),
        P("azim", None, None),
        P(None, "azim", "axial"),
        P(None, "azim", "axial"),
        P("azim", "axial", None),
        P("azim", "axial", None),
        P("azim", "axial", None),
    )
    return jax.shard_map(
        shards,
        mesh=mesh,
        in_specs=placed,
        out_specs=(
            P("azim", "axial", None),
            P("azim", "axial", None),
            P("azim", "axial", None),
            P("azim", "axial", None),
        ),
        check_vma=False,
    )
```

profile of v0, /device:TPU:25, one launch (start us, length us, event | category | flops | bytes accessed | tf_op | source)
XLA Modules:
  0.0 291.4 jit_solution(16157686865284336224)
XLA Ops:
  2.0 2.6 multiply_bitcast_fusion.1
  5.1 1.1 copy.68
  6.2 10.7 %all-to-all-start = ((f32[32,16,256]{2,0,1:T(8,128)}), f32[32,16,256]{2,0,1:T(8,128)S(1)}, u32[]{:S(2)}, u32[]{:S(2)}) async-start(f32[32,16,256]{2,0,1:T(8,128)} %copy.68), calls=%async_computation | async-start | bytes 1048576 | tf_op jit(solution)/shard_map/all_to_all | solution.py:111
  17.0 17.2 %all-to-all-done = f32[32,16,256]{2,0,1:T(8,128)S(1)} async-done(((f32[32,16,256]{2,0,1:T(8,128)}), f32[32,16,256]{2,0,1:T(8,128)S(1)}, u32[]{:S(2)}, u32[]{:S(2)}) %all-to-all-start) | async-done | bytes 524320 | tf_op jit(solution)/shard_map/all_to_all | solution.py:111
  34.2 8.6 %fusion.14 = f32[16,32,256]{2,1,0:T(8,128)} fusion(f32[512,256,1]{1,0,2:T(8,128)S(1)} %bitcast.139, s32[16,32]{1,0:T(8,128)S(1)} %add_select_fusion.2, pred[16,32]{1,0:T(8,128)(4,1)S(1)} %fusion.99), kind=kOutput, calls=%fused_computation.24 | convolution fusion | flops 809238528 | bytes 1051136 | tf_op jit(solution)/shard_map/dot_general | solution.py:113
  42.8 4.7 %all-to-all-start.1 = ((f32[16,32,256]{2,1,0:T(8,128)}), f32[16,32,256]{2,1,0:T(8,128)S(1)}, u32[]{:S(2)}, u32[]{:S(2)}) async-start(f32[16,32,256]{2,1,0:T(8,128)} %fusion.14), calls=%async_computation.1 | async-start | bytes 1048576 | tf_op jit(solution)/shard_map/all_to_all | solution.py:114
  47.6 17.2 %all-to-all-done.1 = f32[16,32,256]{2,1,0:T(8,128)S(1)} async-done(((f32[16,32,256]{2,1,0:T(8,128)}), f32[16,32,256]{2,1,0:T(8,128)S(1)}, u32[]{:S(2)}, u32[]{:S(2)}) %all-to-all-start.1) | async-done | bytes 524320 | tf_op jit(solution)/shard_map/all_to_all | solution.py:114
  65.3 4.3 %collective-permute-start = (f32[32,1,128]{2,1,0:T(1,128)S(1)}, f32[32,1,128]{2,1,0:T(1,128)S(1)}, u32[]{:S(2)}, u32[]{:S(2)}) collective-permute-start(f32[32,1,128]{2,1,0:T(1,128)S(1)} %get-tuple-element.45), channel_id=1, source_target_pairs={{16,0},{32,16},{48,32},{64,48},{80,64},{96,80},{112,96},{128,112},... | collective-permute-start | bytes 49160 | tf_op jit(solution)/shard_map/ppermute | solution.py:31
  69.6 3.4 %collective-permute-start.1 = (f32[32,1,128]{2,1,0:T(1,128)S(1)}, f32[32,1,128]{2,1,0:T(1,128)S(1)}, u32[]{:S(2)}, u32[]{:S(2)}) collective-permute-start(f32[32,1,128]{2,1,0:T(1,128)S(1)} %get-tuple-element.46), channel_id=1, source_target_pairs={{0,16},{16,32},{32,48},{48,64},{64,80},{80,96},{96,112},{112,128},... | collective-permute-start | bytes 49160 | tf_op jit(solution)/shard_map/ppermute | solution.py:28
  74.1 2.7 collective-permute-start.2
  76.8 5.5 %collective-permute-start.3 = (f32[32,1,128]{2,1,0:T(1,128)S(1)}, f32[32,1,128]{2,1,0:T(1,128)S(1)}, u32[]{:S(2)}, u32[]{:S(2)}) collective-permute-start(f32[32,1,128]{2,1,0:T(1,128)S(1)} %get-tuple-element.44), channel_id=1, source_target_pairs={{0,16},{16,32},{32,48},{48,64},{64,80},{80,96},{96,112},{112,128},... | collective-permute-start | bytes 49160 | tf_op jit(solution)/shard_map/ppermute | solution.py:28
  83.4 1.9 collective-permute-start.4
  85.4 6.3 %collective-permute-start.5 = (f32[32,1,128]{2,1,0:T(1,128)S(1)}, f32[32,1,128]{2,1,0:T(1,128)S(1)}, u32[]{:S(2)}, u32[]{:S(2)}) collective-permute-start(f32[32,1,128]{2,1,0:T(1,128)S(1)} %get-tuple-element.42), channel_id=1, source_target_pairs={{0,16},{16,32},{32,48},{48,64},{64,80},{80,96},{96,112},{112,128},... | collective-permute-start | bytes 49160 | tf_op jit(solution)/shard_map/ppermute | solution.py:28
  93.5 4.2 %all-to-all-start.2 = ((f32[32,16,128]{2,0,1:T(8,128)}), f32[32,16,128]{2,0,1:T(8,128)S(1)}, u32[]{:S(2)}, u32[]{:S(2)}) async-start(f32[32,16,128]{2,0,1:T(8,128)} %copy.71), calls=%async_computation.2 | async-start | bytes 524288 | tf_op jit(solution)/shard_map/all_to_all | solution.py:111
  97.7 11.1 %all-to-all-done.2 = f32[32,16,128]{2,0,1:T(8,128)S(1)} async-done(((f32[32,16,128]{2,0,1:T(8,128)}), f32[32,16,128]{2,0,1:T(8,128)S(1)}, u32[]{:S(2)}, u32[]{:S(2)}) %all-to-all-start.2) | async-done | bytes 262176 | tf_op jit(solution)/shard_map/all_to_all | solution.py:111
  108.8 5.1 %fusion.22 = f32[16,32,128]{2,1,0:T(8,128)S(1)} fusion(f32[512,128,1]{1,0,2:T(8,128)S(1)} %bitcast.142, f32[512]{0:T(512)S(1)} %fusion.101, s32[512]{0:T(512)S(1)} %add_select_fusion.3, s32[16,32]{1,0:T(8,128)S(1)} %multiply_add_fusion.3, pred[512]{0:T(512)(128)(4,1)S(1)} %iota_compare_fusion.4), kind=kOutput, calls=%fused_computation.52 | convolution fusion | flops 406847488 | bytes 530944 | tf_op jit(solution)/shard_map/dot_general | solution.py:113
  114.0 14.8 %all_to_all.122 = f32[16,32,128]{2,1,0:T(8,128)S(1)} all-to-all(f32[16,32,128]{2,1,0:T(8,128)S(1)} %fusion.22), channel_id=1, replica_groups=mesh['axial'=16,'azim'=16] {'azim'}, dimensions={0} | all-to-all | bytes 524288 | tf_op jit(solution)/shard_map/all_to_all | solution.py:114
  129.6 21.7 %all_to_all.123 = f32[32,16,256]{2,0,1:T(8,128)S(1)} all-to-all(f32[32,16,256]{2,0,1:T(8,128)S(1)} %copy.73), channel_id=1, replica_groups=mesh['axial'=16,'azim'=16] {'azim'}, dimensions={1} | all-to-all | bytes 1048576 | tf_op jit(solution)/shard_map/all_to_all | solution.py:111
  151.3 8.0 %fusion.12 = f32[16,32,256]{2,1,0:T(8,128)S(1)} fusion(f32[512,256,1]{1,0,2:T(8,128)S(1)} %bitcast.140, s32[16,32]{1,0:T(8,128)S(1)} %add_select_fusion.2, pred[16,32]{1,0:T(8,128)(4,1)S(1)} %fusion.99), kind=kOutput, calls=%fused_computation.22 | convolution fusion | flops 809238528 | bytes 1051136 | tf_op jit(solution)/shard_map/dot_general | solution.py:113
  159.3 20.4 %all_to_all.124 = f32[16,32,256]{2,1,0:T(8,128)S(1)} all-to-all(f32[16,32,256]{2,1,0:T(8,128)S(1)} %fusion.12), channel_id=1, replica_groups=mesh['axial'=16,'azim'=16] {'azim'}, dimensions={0} | all-to-all | bytes 1048576 | tf_op jit(solution)/shard_map/all_to_all | solution.py:114
  180.1 4.5 %collective-permute-start.6 = (f32[32,1,128]{2,1,0:T(1,128)S(1)}, f32[32,1,128]{2,1,0:T(1,128)S(1)}, u32[]{:S(2)}, u32[]{:S(2)}) collective-permute-start(f32[32,1,128]{2,1,0:T(1,128)S(1)} %get-tuple-element.39), channel_id=1, source_target_pairs={{16,0},{32,16},{48,32},{64,48},{80,64},{96,80},{112,96},{128,112},... | collective-permute-start | bytes 49160 | tf_op jit(solution)/shard_map/ppermute | solution.py:31
  184.6 3.2 %collective-permute-start.7 = (f32[32,1,128]{2,1,0:T(1,128)S(1)}, f32[32,1,128]{2,1,0:T(1,128)S(1)}, u32[]{:S(2)}, u32[]{:S(2)}) collective-permute-start(f32[32,1,128]{2,1,0:T(1,128)S(1)} %get-tuple-element.40), channel_id=1, source_target_pairs={{0,16},{16,32},{32,48},{48,64},{64,80},{80,96},{96,112},{112,128},... | collective-permute-start | bytes 49160 | tf_op jit(solution)/shard_map/ppermute | solution.py:28
  188.9 3.0 %collective-permute-start.8 = (f32[32,1,128]{2,1,0:T(1,128)S(1)}, f32[32,1,128]{2,1,0:T(1,128)S(1)}, u32[]{:S(2)}, u32[]{:S(2)}) collective-permute-start(f32[32,1,128]{2,1,0:T(1,128)S(1)} %get-tuple-element.37), channel_id=1, source_target_pairs={{16,0},{32,16},{48,32},{64,48},{80,64},{96,80},{112,96},{128,112},... | collective-permute-start | bytes 49160 | tf_op jit(solution)/shard_map/ppermute | solution.py:31
  191.8 5.3 %collective-permute-start.9 = (f32[32,1,128]{2,1,0:T(1,128)S(1)}, f32[32,1,128]{2,1,0:T(1,128)S(1)}, u32[]{:S(2)}, u32[]{:S(2)}) collective-permute-start(f32[32,1,128]{2,1,0:T(1,128)S(1)} %get-tuple-element.38), channel_id=1, source_target_pairs={{0,16},{16,32},{32,48},{48,64},{64,80},{80,96},{96,112},{112,128},... | collective-permute-start | bytes 49160 | tf_op jit(solution)/shard_map/ppermute | solution.py:28
  198.2 1.9 collective-permute-start.10
  200.1 6.3 %collective-permute-start.11 = (f32[32,1,128]{2,1,0:T(1,128)S(1)}, f32[32,1,128]{2,1,0:T(1,128)S(1)}, u32[]{:S(2)}, u32[]{:S(2)}) collective-permute-start(f32[32,1,128]{2,1,0:T(1,128)S(1)} %get-tuple-element.36), channel_id=1, source_target_pairs={{0,16},{16,32},{32,48},{48,64},{64,80},{80,96},{96,112},{112,128},... | collective-permute-start | bytes 49160 | tf_op jit(solution)/shard_map/ppermute | solution.py:28
  208.3 4.2 %all-to-all-start.6 = ((f32[32,16,128]{2,0,1:T(8,128)}), f32[32,16,128]{2,0,1:T(8,128)S(1)}, u32[]{:S(2)}, u32[]{:S(2)}) async-start(f32[32,16,128]{2,0,1:T(8,128)} %copy.77), calls=%async_computation.6 | async-start | bytes 524288 | tf_op jit(solution)/shard_map/all_to_all | solution.py:111
  212.6 11.1 %all-to-all-done.6 = f32[32,16,128]{2,0,1:T(8,128)S(1)} async-done(((f32[32,16,128]{2,0,1:T(8,128)}), f32[32,16,128]{2,0,1:T(8,128)S(1)}, u32[]{:S(2)}, u32[]{:S(2)}) %all-to-all-start.6) | async-done | bytes 262176 | tf_op jit(solution)/shard_map/all_to_all | solution.py:111
  223.7 6.8 %fusion.21 = f32[16,32,128]{2,1,0:T(8,128)} fusion(f32[512,128,1]{1,0,2:T(8,128)S(1)} %bitcast.141, f32[512]{0:T(512)S(1)} %fusion.101, s32[512]{0:T(512)S(1)} %add_select_fusion.3, s32[16,32]{1,0:T(8,128)S(1)} %multiply_add_fusion.3, pred[512]{0:T(512)(128)(4,1)S(1)} %iota_compare_fusion.4), kind=kOutput, calls=%fused_computation.51 | convolution fusion | flops 406847488 | bytes 530944 | tf_op jit(solution)/shard_map/dot_general | solution.py:113
  230.5 3.7 %all-to-all-start.7 = ((f32[16,32,128]{2,1,0:T(8,128)}), f32[16,32,128]{2,1,0:T(8,128)S(1)}, u32[]{:S(2)}, u32[]{:S(2)}) async-start(f32[16,32,128]{2,1,0:T(8,128)} %fusion.21), calls=%async_computation.7 | async-start | bytes 524288 | tf_op jit(solution)/shard_map/all_to_all | solution.py:114
  234.2 1.9 collective-permute-start.12
  236.2 7.9 %collective-permute-start.13 = (f32[32,1,128]{2,0,1:T(8,128)S(1)}, f32[32,1,128]{2,0,1:T(8,128)S(1)}, u32[]{:S(2)}, u32[]{:S(2)}) collective-permute-start(f32[32,1,128]{2,0,1:T(8,128)S(1)} %get-tuple-element.33), channel_id=1, source_target_pairs={{0,16},{16,32},{32,48},{48,64},{64,80},{80,96},{96,112},{112,128},... | collective-permute-start | bytes 49160 | tf_op jit(solution)/shard_map/ppermute | solution.py:28
  244.2 2.1 all-to-all-done.7
  246.3 1.9 collective-permute-start.16
  248.2 8.1 %collective-permute-start.17 = (f32[32,1,128]{2,0,1:T(8,128)S(1)}, f32[32,1,128]{2,0,1:T(8,128)S(1)}, u32[]{:S(2)}, u32[]{:S(2)}) collective-permute-start(f32[32,1,128]{2,0,1:T(8,128)S(1)} %get-tuple-element.29), channel_id=1, source_target_pairs={{0,16},{16,32},{32,48},{48,64},{64,80},{80,96},{96,112},{112,128},... | collective-permute-start | bytes 49160 | tf_op jit(solution)/shard_map/ppermute | solution.py:28
  256.7 0.9 copy.89
  257.6 0.9 fusion.51
  258.8 5.9 %collective-permute-start.18 = (f32[32,16,128]{2,0,1:T(8,128)S(1)}, f32[32,16,128]{2,0,1:T(8,128)S(1)}, u32[]{:S(2)}, u32[]{:S(2)}) collective-permute-start(f32[32,16,128]{2,0,1:T(8,128)S(1)} %fusion.70), channel_id=1, source_target_pairs={{0,16},{16,32},{32,48},{48,64},{64,80},{80,96},{96,112},{112,128},... | collective-permute-start | bytes 786440 | tf_op jit(solution)/shard_map/ppermute | solution.py:39
  265.1 1.9 collective-permute-start.19
  267.4 5.8 %collective-permute-start.14 = (f32[32,16,128]{2,0,1:T(8,128)S(1)}, f32[32,16,128]{2,0,1:T(8,128)S(1)}, u32[]{:S(2)}, u32[]{:S(2)}) collective-permute-start(f32[32,16,128]{2,0,1:T(8,128)S(1)} %fusion.75), channel_id=1, source_target_pairs={{0,16},{16,32},{32,48},{48,64},{64,80},{80,96},{96,112},{112,128},... | collective-permute-start | bytes 786440 | tf_op jit(solution)/shard_map/ppermute | solution.py:39
  273.5 2.1 collective-permute-start.15
  276.4 1.9 fusion.8
  278.9 4.5 %collective-permute-done.15 = f32[32,16,128]{2,0,1:T(8,128)} collective-permute-done((f32[32,16,128]{2,0,1:T(8,128)S(1)}, f32[32,16,128]{2,0,1:T(8,128)}, u32[]{:S(2)}, u32[]{:S(2)}) %collective-permute-start.15) | collective-permute-done | bytes 262176 | tf_op jit(solution)/shard_map/ppermute | solution.py:39
  283.4 1.3 fusion.1
  285.1 1.9 fusion.10
  288.8 0.9 copy.90
  289.7 0.9 copy.91
  290.5 0.9 copy.92
  (95 shorter events, 16.9 us)
Async XLA Ops:
  0.6 275.8 %copy-start = (f32[32,64,64]{2,1,0:T(8,128)S(1)}, f32[32,64,64]{2,1,0:T(8,128)}, u32[]{:S(2)}) copy-start(f32[32,64,64]{2,1,0:T(8,128)} %param.14) | copy-start | bytes 1572868
  0.6 0.7 copy-start.5
  6.2 28.0 %all-to-all-start = ((f32[32,16,256]{2,0,1:T(8,128)}), f32[32,16,256]{2,0,1:T(8,128)S(1)}, u32[]{:S(2)}, u32[]{:S(2)}) async-start(f32[32,16,256]{2,0,1:T(8,128)} %copy.68), calls=%async_computation | async-start | bytes 1048576 | tf_op jit(solution)/shard_map/all_to_all | solution.py:111
  42.8 22.0 %all-to-all-start.1 = ((f32[16,32,256]{2,1,0:T(8,128)}), f32[16,32,256]{2,1,0:T(8,128)S(1)}, u32[]{:S(2)}, u32[]{:S(2)}) async-start(f32[16,32,256]{2,1,0:T(8,128)} %fusion.14), calls=%async_computation.1 | async-start | bytes 1048576 | tf_op jit(solution)/shard_map/all_to_all | solution.py:114
  65.3 7.7 %collective-permute-start = (f32[32,1,128]{2,1,0:T(1,128)S(1)}, f32[32,1,128]{2,1,0:T(1,128)S(1)}, u32[]{:S(2)}, u32[]{:S(2)}) collective-permute-start(f32[32,1,128]{2,1,0:T(1,128)S(1)} %get-tuple-element.45), channel_id=1, source_target_pairs={{16,0},{32,16},{48,32},{64,48},{80,64},{96,80},{112,96},{128,112},... | collective-permute-start | bytes 49160 | tf_op jit(solution)/shard_map/ppermute | solution.py:31
  69.6 4.3 %collective-permute-start.1 = (f32[32,1,128]{2,1,0:T(1,128)S(1)}, f32[32,1,128]{2,1,0:T(1,128)S(1)}, u32[]{:S(2)}, u32[]{:S(2)}) collective-permute-start(f32[32,1,128]{2,1,0:T(1,128)S(1)} %get-tuple-element.46), channel_id=1, source_target_pairs={{0,16},{16,32},{32,48},{48,64},{64,80},{80,96},{96,112},{112,128},... | collective-permute-start | bytes 49160 | tf_op jit(solution)/shard_map/ppermute | solution.py:28
  74.1 8.3 %collective-permute-start.2 = (f32[32,1,128]{2,1,0:T(1,128)S(1)}, f32[32,1,128]{2,1,0:T(1,128)S(1)}, u32[]{:S(2)}, u32[]{:S(2)}) collective-permute-start(f32[32,1,128]{2,1,0:T(1,128)S(1)} %get-tuple-element.43), channel_id=1, source_target_pairs={{16,0},{32,16},{48,32},{64,48},{80,64},{96,80},{112,96},{128,112},... | collective-permute-start | bytes 49160 | tf_op jit(solution)/shard_map/ppermute | solution.py:31
  76.8 6.4 %collective-permute-start.3 = (f32[32,1,128]{2,1,0:T(1,128)S(1)}, f32[32,1,128]{2,1,0:T(1,128)S(1)}, u32[]{:S(2)}, u32[]{:S(2)}) collective-permute-start(f32[32,1,128]{2,1,0:T(1,128)S(1)} %get-tuple-element.44), channel_id=1, source_target_pairs={{0,16},{16,32},{32,48},{48,64},{64,80},{80,96},{96,112},{112,128},... | collective-permute-start | bytes 49160 | tf_op jit(solution)/shard_map/ppermute | solution.py:28
  83.4 8.3 %collective-permute-start.4 = (f32[32,1,128]{2,1,0:T(1,128)S(1)}, f32[32,1,128]{2,1,0:T(1,128)S(1)}, u32[]{:S(2)}, u32[]{:S(2)}) collective-permute-start(f32[32,1,128]{2,1,0:T(1,128)S(1)} %get-tuple-element.41), channel_id=1, source_target_pairs={{16,0},{32,16},{48,32},{64,48},{80,64},{96,80},{112,96},{128,112},... | collective-permute-start | bytes 49160 | tf_op jit(solution)/shard_map/ppermute | solution.py:31
  85.4 7.2 %collective-permute-start.5 = (f32[32,1,128]{2,1,0:T(1,128)S(1)}, f32[32,1,128]{2,1,0:T(1,128)S(1)}, u32[]{:S(2)}, u32[]{:S(2)}) collective-permute-start(f32[32,1,128]{2,1,0:T(1,128)S(1)} %get-tuple-element.42), channel_id=1, source_target_pairs={{0,16},{16,32},{32,48},{48,64},{64,80},{80,96},{96,112},{112,128},... | collective-permute-start | bytes 49160 | tf_op jit(solution)/shard_map/ppermute | solution.py:28
  93.5 15.3 %all-to-all-start.2 = ((f32[32,16,128]{2,0,1:T(8,128)}), f32[32,16,128]{2,0,1:T(8,128)S(1)}, u32[]{:S(2)}, u32[]{:S(2)}) async-start(f32[32,16,128]{2,0,1:T(8,128)} %copy.71), calls=%async_computation.2 | async-start | bytes 524288 | tf_op jit(solution)/shard_map/all_to_all | solution.py:111
  180.1 7.7 %collective-permute-start.6 = (f32[32,1,128]{2,1,0:T(1,128)S(1)}, f32[32,1,128]{2,1,0:T(1,128)S(1)}, u32[]{:S(2)}, u32[]{:S(2)}) collective-permute-start(f32[32,1,128]{2,1,0:T(1,128)S(1)} %get-tuple-element.39), channel_id=1, source_target_pairs={{16,0},{32,16},{48,32},{64,48},{80,64},{96,80},{112,96},{128,112},... | collective-permute-start | bytes 49160 | tf_op jit(solution)/shard_map/ppermute | solution.py:31
  184.6 4.0 %collective-permute-start.7 = (f32[32,1,128]{2,1,0:T(1,128)S(1)}, f32[32,1,128]{2,1,0:T(1,128)S(1)}, u32[]{:S(2)}, u32[]{:S(2)}) collective-permute-start(f32[32,1,128]{2,1,0:T(1,128)S(1)} %get-tuple-element.40), channel_id=1, source_target_pairs={{0,16},{16,32},{32,48},{48,64},{64,80},{80,96},{96,112},{112,128},... | collective-permute-start | bytes 49160 | tf_op jit(solution)/shard_map/ppermute | solution.py:28
  188.9 8.3 %collective-permute-start.8 = (f32[32,1,128]{2,1,0:T(1,128)S(1)}, f32[32,1,128]{2,1,0:T(1,128)S(1)}, u32[]{:S(2)}, u32[]{:S(2)}) collective-permute-start(f32[32,1,128]{2,1,0:T(1,128)S(1)} %get-tuple-element.37), channel_id=1, source_target_pairs={{16,0},{32,16},{48,32},{64,48},{80,64},{96,80},{112,96},{128,112},... | collective-permute-start | bytes 49160 | tf_op jit(solution)/shard_map/ppermute | solution.py:31
  191.8 6.1 %collective-permute-start.9 = (f32[32,1,128]{2,1,0:T(1,128)S(1)}, f32[32,1,128]{2,1,0:T(1,128)S(1)}, u32[]{:S(2)}, u32[]{:S(2)}) collective-permute-start(f32[32,1,128]{2,1,0:T(1,128)S(1)} %get-tuple-element.38), channel_id=1, source_target_pairs={{0,16},{16,32},{32,48},{48,64},{64,80},{80,96},{96,112},{112,128},... | collective-permute-start | bytes 49160 | tf_op jit(solution)/shard_map/ppermute | solution.py:28
  198.2 8.3 %collective-permute-start.10 = (f32[32,1,128]{2,1,0:T(1,128)S(1)}, f32[32,1,128]{2,1,0:T(1,128)S(1)}, u32[]{:S(2)}, u32[]{:S(2)}) collective-permute-start(f32[32,1,128]{2,1,0:T(1,128)S(1)} %get-tuple-element.35), channel_id=1, source_target_pairs={{16,0},{32,16},{48,32},{64,48},{80,64},{96,80},{112,96},{128,112},... | collective-permute-start | bytes 49160 | tf_op jit(solution)/shard_map/ppermute | solution.py:31
  200.1 7.2 %collective-permute-start.11 = (f32[32,1,128]{2,1,0:T(1,128)S(1)}, f32[32,1,128]{2,1,0:T(1,128)S(1)}, u32[]{:S(2)}, u32[]{:S(2)}) collective-permute-start(f32[32,1,128]{2,1,0:T(1,128)S(1)} %get-tuple-element.36), channel_id=1, source_target_pairs={{0,16},{16,32},{32,48},{48,64},{64,80},{80,96},{96,112},{112,128},... | collective-permute-start | bytes 49160 | tf_op jit(solution)/shard_map/ppermute | solution.py:28
  208.3 4.3 %copy-start.7 = (s32[2,32,1]{1,2,0:T(1,128)S(1)}, s32[2,32,1]{1,2,0:T(1,128)}, u32[]{:S(2)}) copy-start(s32[2,32,1]{1,2,0:T(1,128)} %param.15) | copy-start | bytes 772
  208.3 15.4 %all-to-all-start.6 = ((f32[32,16,128]{2,0,1:T(8,128)}), f32[32,16,128]{2,0,1:T(8,128)S(1)}, u32[]{:S(2)}, u32[]{:S(2)}) async-start(f32[32,16,128]{2,0,1:T(8,128)} %copy.77), calls=%async_computation.6 | async-start | bytes 524288 | tf_op jit(solution)/shard_map/all_to_all | solution.py:111
  230.5 3.7 %copy-start.6 = (s32[2,32,1]{1,2,0:T(1,128)S(1)}, s32[2,32,1]{1,2,0:T(1,128)}, u32[]{:S(2)}) copy-start(s32[2,32,1]{1,2,0:T(1,128)} %param.16) | copy-start | bytes 772
  230.5 15.8 %all-to-all-start.7 = ((f32[16,32,128]{2,1,0:T(8,128)}), f32[16,32,128]{2,1,0:T(8,128)S(1)}, u32[]{:S(2)}, u32[]{:S(2)}) async-start(f32[16,32,128]{2,1,0:T(8,128)} %fusion.21), calls=%async_computation.7 | async-start | bytes 524288 | tf_op jit(solution)/shard_map/all_to_all | solution.py:114
  234.2 23.3 %collective-permute-start.12 = (f32[32,1,128]{2,0,1:T(8,128)S(1)}, f32[32,1,128]{2,0,1:T(8,128)S(1)}, u32[]{:S(2)}, u32[]{:S(2)}) collective-permute-start(f32[32,1,128]{2,0,1:T(8,128)S(1)} %get-tuple-element.34), channel_id=1, source_target_pairs={{16,0},{32,16},{48,32},{64,48},{80,64},{96,80},{112,96},{128,112},... | collective-permute-start | bytes 49160 | tf_op jit(solution)/shard_map/ppermute | solution.py:31
  236.1 20.2 %copy-start.1 = (f32[32,16,128]{2,1,0:T(8,128)S(1)}, f32[32,16,128]{2,1,0:T(8,128)}, u32[]{:S(2)}) copy-start(f32[32,16,128]{2,1,0:T(8,128)} %param.13) | copy-start | bytes 786436
  236.2 21.4 %collective-permute-start.13 = (f32[32,1,128]{2,0,1:T(8,128)S(1)}, f32[32,1,128]{2,0,1:T(8,128)S(1)}, u32[]{:S(2)}, u32[]{:S(2)}) collective-permute-start(f32[32,1,128]{2,0,1:T(8,128)S(1)} %get-tuple-element.33), channel_id=1, source_target_pairs={{0,16},{16,32},{32,48},{48,64},{64,80},{80,96},{96,112},{112,128},... | collective-permute-start | bytes 49160 | tf_op jit(solution)/shard_map/ppermute | solution.py:28
  246.3 11.3 %collective-permute-start.16 = (f32[32,1,128]{2,0,1:T(8,128)S(1)}, f32[32,1,128]{2,0,1:T(8,128)S(1)}, u32[]{:S(2)}, u32[]{:S(2)}) collective-permute-start(f32[32,1,128]{2,0,1:T(8,128)S(1)} %get-tuple-element.30), channel_id=1, source_target_pairs={{16,0},{32,16},{48,32},{64,48},{80,64},{96,80},{112,96},{128,112},... | collective-permute-start | bytes 49160 | tf_op jit(solution)/shard_map/ppermute | solution.py:31
  248.2 9.3 %collective-permute-start.17 = (f32[32,1,128]{2,0,1:T(8,128)S(1)}, f32[32,1,128]{2,0,1:T(8,128)S(1)}, u32[]{:S(2)}, u32[]{:S(2)}) collective-permute-start(f32[32,1,128]{2,0,1:T(8,128)S(1)} %get-tuple-element.29), channel_id=1, source_target_pairs={{0,16},{16,32},{32,48},{48,64},{64,80},{80,96},{96,112},{112,128},... | collective-permute-start | bytes 49160 | tf_op jit(solution)/shard_map/ppermute | solution.py:28
  258.8 16.9 %collective-permute-start.18 = (f32[32,16,128]{2,0,1:T(8,128)S(1)}, f32[32,16,128]{2,0,1:T(8,128)S(1)}, u32[]{:S(2)}, u32[]{:S(2)}) collective-permute-start(f32[32,16,128]{2,0,1:T(8,128)S(1)} %fusion.70), channel_id=1, source_target_pairs={{0,16},{16,32},{32,48},{48,64},{64,80},{80,96},{96,112},{112,128},... | collective-permute-start | bytes 786440 | tf_op jit(solution)/shard_map/ppermute | solution.py:39
  265.1 10.6 %collective-permute-start.19 = (f32[32,16,128]{2,0,1:T(8,128)S(1)}, f32[32,16,128]{2,0,1:T(8,128)S(1)}, u32[]{:S(2)}, u32[]{:S(2)}) collective-permute-start(f32[32,16,128]{2,0,1:T(8,128)S(1)} %fusion.68), channel_id=1, source_target_pairs={{16,0},{32,16},{48,32},{64,48},{80,64},{96,80},{112,96},{128,112},... | collective-permute-start | bytes 786440 | tf_op jit(solution)/shard_map/ppermute | solution.py:39
  267.4 11.5 %collective-permute-start.14 = (f32[32,16,128]{2,0,1:T(8,128)S(1)}, f32[32,16,128]{2,0,1:T(8,128)S(1)}, u32[]{:S(2)}, u32[]{:S(2)}) collective-permute-start(f32[32,16,128]{2,0,1:T(8,128)S(1)} %fusion.75), channel_id=1, source_target_pairs={{0,16},{16,32},{32,48},{48,64},{64,80},{80,96},{96,112},{112,128},... | collective-permute-start | bytes 786440 | tf_op jit(solution)/shard_map/ppermute | solution.py:39
  273.5 9.9 %collective-permute-start.15 = (f32[32,16,128]{2,0,1:T(8,128)S(1)}, f32[32,16,128]{2,0,1:T(8,128)}, u32[]{:S(2)}, u32[]{:S(2)}) collective-permute-start(f32[32,16,128]{2,0,1:T(8,128)S(1)} %fusion.73), channel_id=1, source_target_pairs={{16,0},{32,16},{48,32},{64,48},{80,64},{96,80},{112,96},{128,112},... | collective-permute-start | bytes 786440 | tf_op jit(solution)/shard_map/ppermute | solution.py:39
  287.3 1.0 copy-start.2
  287.3 1.0 copy-start.3
  287.3 1.1 copy-start.4
where the time goes:
time: 293 us; the launch traced here: 291 us
  starting transfers between devices  111 us (38%)
  waiting for transfers between devices  68.2 us (23%)
  blocking collectives  56.9 us (19%)
  matrix products  35.4 us (12%)
  local copies, waits for them, and re-layouts  12.6 us (4%)
  other arithmetic  5.6 us (2%)
    ppermute x8, starting transfers between devices, with_halo(): lax.ppermute(lax.slice_in_dim(block, block.shape[dim] - width, None, axis...  45.9 us
    all_to_all x3, waiting for transfers between devices, transform(): lax.all_to_all(columns_all, 'azim', split_axis=1, concat_axis=0, tiled=True)  39.3 us
    all_to_all x2, blocking collectives, transform(): lax.all_to_all(mixed, 'azim', split_axis=0, concat_axis=1, tiled=True)  35.2 us
    dot_general x4, matrix products, transform(): jnp.dot(full_table.T, spread, precision=HIGH, preferred_element_type=jnp....  28.5 us
    ppermute x8, starting transfers between devices, with_halo(): lax.ppermute(lax.slice_in_dim(block, 0, width, axis=dim), axis, backward)  22.1 us
    all_to_all x1, blocking collectives, transform(): lax.all_to_all(columns_all, 'azim', split_axis=1, concat_axis=0, tiled=True)  21.7 us
    all_to_all x2, waiting for transfers between devices, transform(): lax.all_to_all(mixed, 'azim', split_axis=0, concat_axis=1, tiled=True)  19.3 us
    all_to_all x3, starting transfers between devices, transform(): lax.all_to_all(columns_all, 'azim', split_axis=1, concat_axis=0, tiled=True)  19.2 us
  transfers between devices with their start and end apart: 25, of which 12 were waited for; matrix products, arithmetic and copies ran while one was open for 2% of the time, Pallas kernels for 0%

commit v1 on v0

--- a/solution.py
+++ b/solution.py
@@ -108,7 +108,10 @@
 def transform(parts, table_rows, all_index):
     flat_shape = parts.shape
     columns_all = parts.reshape(flat_shape[0], -1)
-    spread = lax.all_to_all(columns_all, "azim", split_axis=1, concat_axis=0, tiled=True)
+    size = lax.axis_size("azim")
+    blocks = jnp.stack(jnp.split(columns_all, size, axis=1), axis=0)
+    blocks = lax.all_to_all(blocks, "azim", split_axis=0, concat_axis=0)
+    spread = jnp.concatenate(blocks, axis=0)
     full_table = table_rows(all_index, all_index)
     mixed = jnp.dot(full_table.T, spread, precision=HIGH, preferred_element_type=jnp.float32)
     joined = lax.all_to_all(mixed, "azim", split_axis=0, concat_axis=1, tiled=True)

time: 293 us -> 320 us (1.092)
  local copies, waits for them, and re-layouts: 12.6 us -> 39.3 us
    unnamed x20 -> x84, local copies, waits for them, and re-layouts: 4.97 us -> 33.1 us
where the time goes in v1:
time: 320 us; the launch traced here: 318 us
  starting transfers between devices  111 us (35%)
  waiting for transfers between devices  68.2 us (21%)
  blocking collectives  56.9 us (18%)
  local copies, waits for them, and re-layouts  39.3 us (12%)
  matrix products  35.4 us (11%)
  other arithmetic  5.6 us (2%)
    ppermute x8, starting transfers between devices, with_halo(): lax.ppermute(lax.slice_in_dim(block, block.shape[dim] - width, None, axis...  46 us
    all_to_all x3, waiting for transfers between devices, transform(): blocks = lax.all_to_all(blocks, 'azim', split_axis=0, concat_axis=0)  39.3 us
    all_to_all x2, blocking collectives, transform(): lax.all_to_all(mixed, 'azim', split_axis=0, concat_axis=1, tiled=True)  35.2 us
    unnamed x84, local copies, waits for them, and re-layouts  33.1 us
    dot_general x4, matrix products, transform(): jnp.dot(full_table.T, spread, precision=HIGH, preferred_element_type=jnp....  28.5 us
    ppermute x8, starting transfers between devices, with_halo(): lax.ppermute(lax.slice_in_dim(block, 0, width, axis=dim), axis, backward)  22.1 us
    all_to_all x1, blocking collectives, transform(): blocks = lax.all_to_all(blocks, 'azim', split_axis=0, concat_axis=0)  21.7 us
    all_to_all x2, waiting for transfers between devices, transform(): lax.all_to_all(mixed, 'azim', split_axis=0, concat_axis=1, tiled=True)  19.3 us
  transfers between devices with their start and end apart: 25, of which 12 were waited for; matrix products, arithmetic and copies ran while one was open for 2% of the time, Pallas kernels for 0%

profile of v1, /device:TPU:25, one launch (start us, length us, event | category | flops | bytes accessed | tf_op | source)
XLA Modules:
  0.0 318.3 jit_solution(3733252265822538703)
XLA Ops:
  2.0 2.6 multiply_bitcast_fusion.1
  15.0 10.7 %all-to-all-start = ((f32[16,32,256]{2,1,0:T(8,128)}), f32[16,32,256]{2,1,0:T(8,128)S(1)}, u32[]{:S(2)}, u32[]{:S(2)}) async-start(f32[16,32,256]{2,1,0:T(8,128)} %constant_dynamic-update-slice_fusion), calls=%async_computation | async-start | bytes 1048576 | tf_op jit(solution)/shard_map/all_to_all | solution.py:113
  25.8 17.2 %all-to-all-done = f32[16,32,256]{2,1,0:T(8,128)S(1)} async-done(((f32[16,32,256]{2,1,0:T(8,128)}), f32[16,32,256]{2,1,0:T(8,128)S(1)}, u32[]{:S(2)}, u32[]{:S(2)}) %all-to-all-start) | async-done | bytes 524320 | tf_op jit(solution)/shard_map/all_to_all | solution.py:113
  43.0 8.6 %fusion.14 = f32[16,32,256]{2,1,0:T(8,128)} fusion(f32[512,256,1]{1,0,2:T(8,128)S(1)} %bitcast.469, s32[16,32]{1,0:T(8,128)S(1)} %add_select_fusion.2, pred[16,32]{1,0:T(8,128)(4,1)S(1)} %fusion.99), kind=kOutput, calls=%fused_computation.24 | convolution fusion | flops 809238528 | bytes 1051136 | tf_op jit(solution)/shard_map/dot_general | solution.py:116
  51.6 4.7 %all-to-all-start.1 = ((f32[16,32,256]{2,1,0:T(8,128)}), f32[16,32,256]{2,1,0:T(8,128)S(1)}, u32[]{:S(2)}, u32[]{:S(2)}) async-start(f32[16,32,256]{2,1,0:T(8,128)} %fusion.14), calls=%async_computation.1 | async-start | bytes 1048576 | tf_op jit(solution)/shard_map/all_to_all | solution.py:117
  56.4 17.2 %all-to-all-done.1 = f32[16,32,256]{2,1,0:T(8,128)S(1)} async-done(((f32[16,32,256]{2,1,0:T(8,128)}), f32[16,32,256]{2,1,0:T(8,128)S(1)}, u32[]{:S(2)}, u32[]{:S(2)}) %all-to-all-start.1) | async-done | bytes 524320 | tf_op jit(solution)/shard_map/all_to_all | solution.py:117
  74.1 4.3 %collective-permute-start = (f32[32,1,128]{2,1,0:T(1,128)S(1)}, f32[32,1,128]{2,1,0:T(1,128)S(1)}, u32[]{:S(2)}, u32[]{:S(2)}) collective-permute-start(f32[32,1,128]{2,1,0:T(1,128)S(1)} %get-tuple-element.41), channel_id=1, source_target_pairs={{16,0},{32,16},{48,32},{64,48},{80,64},{96,80},{112,96},{128,112},... | collective-permute-start | bytes 49160 | tf_op jit(solution)/shard_map/ppermute | solution.py:31
  78.3 3.4 %collective-permute-start.1 = (f32[32,1,128]{2,1,0:T(1,128)S(1)}, f32[32,1,128]{2,1,0:T(1,128)S(1)}, u32[]{:S(2)}, u32[]{:S(2)}) collective-permute-start(f32[32,1,128]{2,1,0:T(1,128)S(1)} %get-tuple-element.42), channel_id=1, source_target_pairs={{0,16},{16,32},{32,48},{48,64},{64,80},{80,96},{96,112},{112,128},... | collective-permute-start | bytes 49160 | tf_op jit(solution)/shard_map/ppermute | solution.py:28
  82.9 2.7 collective-permute-start.2
  85.6 5.5 %collective-permute-start.3 = (f32[32,1,128]{2,1,0:T(1,128)S(1)}, f32[32,1,128]{2,1,0:T(1,128)S(1)}, u32[]{:S(2)}, u32[]{:S(2)}) collective-permute-start(f32[32,1,128]{2,1,0:T(1,128)S(1)} %get-tuple-element.40), channel_id=1, source_target_pairs={{0,16},{16,32},{32,48},{48,64},{64,80},{80,96},{96,112},{112,128},... | collective-permute-start | bytes 49160 | tf_op jit(solution)/shard_map/ppermute | solution.py:28
  92.2 1.9 collective-permute-start.4
  94.1 6.3 %collective-permute-start.5 = (f32[32,1,128]{2,1,0:T(1,128)S(1)}, f32[32,1,128]{2,1,0:T(1,128)S(1)}, u32[]{:S(2)}, u32[]{:S(2)}) collective-permute-start(f32[32,1,128]{2,1,0:T(1,128)S(1)} %get-tuple-element.38), channel_id=1, source_target_pairs={{0,16},{16,32},{32,48},{48,64},{64,80},{80,96},{96,112},{112,128},... | collective-permute-start | bytes 49160 | tf_op jit(solution)/shard_map/ppermute | solution.py:28
  111.3 4.2 %all-to-all-start.2 = ((f32[16,32,128]{2,1,0:T(8,128)}), f32[16,32,128]{2,1,0:T(8,128)S(1)}, u32[]{:S(2)}, u32[]{:S(2)}) async-start(f32[16,32,128]{2,1,0:T(8,128)} %constant_dynamic-update-slice_fusion.16), calls=%async_computation.2 | async-start | bytes 524288 | tf_op jit(solution)/shard_map/all_to_all | solution.py:113
  115.5 11.1 %all-to-all-done.2 = f32[16,32,128]{2,1,0:T(8,128)S(1)} async-done(((f32[16,32,128]{2,1,0:T(8,128)}), f32[16,32,128]{2,1,0:T(8,128)S(1)}, u32[]{:S(2)}, u32[]{:S(2)}) %all-to-all-start.2) | async-done | bytes 262176 | tf_op jit(solution)/shard_map/all_to_all | solution.py:113
  126.6 5.1 %fusion.22 = f32[16,32,128]{2,1,0:T(8,128)S(1)} fusion(f32[512,128,1]{1,0,2:T(8,128)S(1)} %bitcast.472, f32[512]{0:T(512)S(1)} %fusion.101, s32[512]{0:T(512)S(1)} %add_select_fusion.3, s32[16,32]{1,0:T(8,128)S(1)} %multiply_add_fusion.3, pred[512]{0:T(512)(128)(4,1)S(1)} %iota_compare_fusion.4), kind=kOutput, calls=%fused_computation.54 | convolution fusion | flops 406847488 | bytes 530944 | tf_op jit(solution)/shard_map/dot_general | solution.py:116
  131.7 14.8 %all_to_all.72 = f32[16,32,128]{2,1,0:T(8,128)S(1)} all-to-all(f32[16,32,128]{2,1,0:T(8,128)S(1)} %fusion.22), channel_id=1, replica_groups=mesh['axial'=16,'azim'=16] {'azim'}, dimensions={0} | all-to-all | bytes 524288 | tf_op jit(solution)/shard_map/all_to_all | solution.py:117
  147.4 21.7 %all_to_all.73 = f32[16,32,256]{2,1,0:T(8,128)S(1)} all-to-all(f32[16,32,256]{2,1,0:T(8,128)S(1)} %constant_dynamic-update-slice_fusion.32), channel_id=1, replica_groups=mesh['axial'=16,'azim'=16] {'azim'}, dimensions={0} | all-to-all | bytes 1048576 | tf_op jit(solution)/shard_map/all_to_all | solution.py:113
  169.1 8.0 %fusion.12 = f32[16,32,256]{2,1,0:T(8,128)S(1)} fusion(f32[512,256,1]{1,0,2:T(8,128)S(1)} %bitcast.470, s32[16,32]{1,0:T(8,128)S(1)} %add_select_fusion.2, pred[16,32]{1,0:T(8,128)(4,1)S(1)} %fusion.99), kind=kOutput, calls=%fused_computation.22 | convolution fusion | flops 809238528 | bytes 1051136 | tf_op jit(solution)/shard_map/dot_general | solution.py:116
  177.1 20.4 %all_to_all.74 = f32[16,32,256]{2,1,0:T(8,128)S(1)} all-to-all(f32[16,32,256]{2,1,0:T(8,128)S(1)} %fusion.12), channel_id=1, replica_groups=mesh['axial'=16,'azim'=16] {'azim'}, dimensions={0} | all-to-all | bytes 1048576 | tf_op jit(solution)/shard_map/all_to_all | solution.py:117
  197.9 4.5 %collective-permute-start.6 = (f32[32,1,128]{2,1,0:T(1,128)S(1)}, f32[32,1,128]{2,1,0:T(1,128)S(1)}, u32[]{:S(2)}, u32[]{:S(2)}) collective-permute-start(f32[32,1,128]{2,1,0:T(1,128)S(1)} %get-tuple-element.35), channel_id=1, source_target_pairs={{16,0},{32,16},{48,32},{64,48},{80,64},{96,80},{112,96},{128,112},... | collective-permute-start | bytes 49160 | tf_op jit(solution)/shard_map/ppermute | solution.py:31
  202.4 3.2 collective-permute-start.7
  206.7 3.0 collective-permute-start.8
  209.7 5.3 %collective-permute-start.9 = (f32[32,1,128]{2,1,0:T(1,128)S(1)}, f32[32,1,128]{2,1,0:T(1,128)S(1)}, u32[]{:S(2)}, u32[]{:S(2)}) collective-permute-start(f32[32,1,128]{2,1,0:T(1,128)S(1)} %get-tuple-element.34), channel_id=1, source_target_pairs={{0,16},{16,32},{32,48},{48,64},{64,80},{80,96},{96,112},{112,128},... | collective-permute-start | bytes 49160 | tf_op jit(solution)/shard_map/ppermute | solution.py:28
  215.0 0.8 collective-permute-done.9
  216.0 1.9 collective-permute-start.10
  218.0 6.3 %collective-permute-start.11 = (f32[32,1,128]{2,1,0:T(1,128)S(1)}, f32[32,1,128]{2,1,0:T(1,128)S(1)}, u32[]{:S(2)}, u32[]{:S(2)}) collective-permute-start(f32[32,1,128]{2,1,0:T(1,128)S(1)} %get-tuple-element.32), channel_id=1, source_target_pairs={{0,16},{16,32},{32,48},{48,64},{64,80},{80,96},{96,112},{112,128},... | collective-permute-start | bytes 49160 | tf_op jit(solution)/shard_map/ppermute | solution.py:28
  235.2 4.2 %all-to-all-start.6 = ((f32[16,32,128]{2,1,0:T(8,128)}), f32[16,32,128]{2,1,0:T(8,128)S(1)}, u32[]{:S(2)}, u32[]{:S(2)}) async-start(f32[16,32,128]{2,1,0:T(8,128)} %constant_dynamic-update-slice_fusion.48), calls=%async_computation.6 | async-start | bytes 524288 | tf_op jit(solution)/shard_map/all_to_all | solution.py:113
  239.5 11.1 %all-to-all-done.6 = f32[16,32,128]{2,1,0:T(8,128)S(1)} async-done(((f32[16,32,128]{2,1,0:T(8,128)}), f32[16,32,128]{2,1,0:T(8,128)S(1)}, u32[]{:S(2)}, u32[]{:S(2)}) %all-to-all-start.6) | async-done | bytes 262176 | tf_op jit(solution)/shard_map/all_to_all | solution.py:113
  250.6 6.8 %fusion.21 = f32[16,32,128]{2,1,0:T(8,128)} fusion(f32[512,128,1]{1,0,2:T(8,128)S(1)} %bitcast.471, f32[512]{0:T(512)S(1)} %fusion.101, s32[512]{0:T(512)S(1)} %add_select_fusion.3, s32[16,32]{1,0:T(8,128)S(1)} %multiply_add_fusion.3, pred[512]{0:T(512)(128)(4,1)S(1)} %iota_compare_fusion.4), kind=kOutput, calls=%fused_computation.53 | convolution fusion | flops 406847488 | bytes 530944 | tf_op jit(solution)/shard_map/dot_general | solution.py:116
  257.3 3.7 %all-to-all-start.7 = ((f32[16,32,128]{2,1,0:T(8,128)}), f32[16,32,128]{2,1,0:T(8,128)S(1)}, u32[]{:S(2)}, u32[]{:S(2)}) async-start(f32[16,32,128]{2,1,0:T(8,128)} %fusion.21), calls=%async_computation.7 | async-start | bytes 524288 | tf_op jit(solution)/shard_map/all_to_all | solution.py:117
  261.1 1.9 collective-permute-start.12
  263.0 7.9 %collective-permute-start.13 = (f32[32,1,128]{2,0,1:T(8,128)S(1)}, f32[32,1,128]{2,0,1:T(8,128)S(1)}, u32[]{:S(2)}, u32[]{:S(2)}) collective-permute-start(f32[32,1,128]{2,0,1:T(8,128)S(1)} %get-tuple-element.29), channel_id=1, source_target_pairs={{0,16},{16,32},{32,48},{48,64},{64,80},{80,96},{96,112},{112,128},... | collective-permute-start | bytes 49160 | tf_op jit(solution)/shard_map/ppermute | solution.py:28
  271.1 2.1 all-to-all-done.7
  273.2 1.9 collective-permute-start.16
  275.1 8.1 %collective-permute-start.17 = (f32[32,1,128]{2,0,1:T(8,128)S(1)}, f32[32,1,128]{2,0,1:T(8,128)S(1)}, u32[]{:S(2)}, u32[]{:S(2)}) collective-permute-start(f32[32,1,128]{2,0,1:T(8,128)S(1)} %get-tuple-element.25), channel_id=1, source_target_pairs={{0,16},{16,32},{32,48},{48,64},{64,80},{80,96},{96,112},{112,128},... | collective-permute-start | bytes 49160 | tf_op jit(solution)/shard_map/ppermute | solution.py:28
  283.6 0.9 copy.55
  284.4 0.9 fusion.51
  285.7 5.9 %collective-permute-start.18 = (f32[32,16,128]{2,0,1:T(8,128)S(1)}, f32[32,16,128]{2,0,1:T(8,128)S(1)}, u32[]{:S(2)}, u32[]{:S(2)}) collective-permute-start(f32[32,16,128]{2,0,1:T(8,128)S(1)} %fusion.70), channel_id=1, source_target_pairs={{0,16},{16,32},{32,48},{48,64},{64,80},{80,96},{96,112},{112,128},... | collective-permute-start | bytes 786440 | tf_op jit(solution)/shard_map/ppermute | solution.py:39
  292.0 1.9 collective-permute-start.19
  294.3 5.8 %collective-permute-start.14 = (f32[32,16,128]{2,0,1:T(8,128)S(1)}, f32[32,16,128]{2,0,1:T(8,128)S(1)}, u32[]{:S(2)}, u32[]{:S(2)}) collective-permute-start(f32[32,16,128]{2,0,1:T(8,128)S(1)} %fusion.75), channel_id=1, source_target_pairs={{0,16},{16,32},{32,48},{48,64},{64,80},{80,96},{96,112},{112,128},... | collective-permute-start | bytes 786440 | tf_op jit(solution)/shard_map/ppermute | solution.py:39
  300.4 2.1 collective-permute-start.15
  303.3 1.9 fusion.8
  305.8 4.5 %collective-permute-done.15 = f32[32,16,128]{2,0,1:T(8,128)} collective-permute-done((f32[32,16,128]{2,0,1:T(8,128)S(1)}, f32[32,16,128]{2,0,1:T(8,128)}, u32[]{:S(2)}, u32[]{:S(2)}) %collective-permute-start.15) | collective-permute-done | bytes 262176 | tf_op jit(solution)/shard_map/ppermute | solution.py:39
  310.3 1.3 fusion.1
  311.9 1.9 fusion.10
  315.7 0.9 copy.56
  316.5 0.9 copy.57
  317.4 0.9 copy.58
  (157 shorter events, 43.9 us)
Async XLA Ops:
  0.6 302.6 %copy-start = (f32[32,64,64]{2,1,0:T(8,128)S(1)}, f32[32,64,64]{2,1,0:T(8,128)}, u32[]{:S(2)}) copy-start(f32[32,64,64]{2,1,0:T(8,128)} %param.14) | copy-start | bytes 1572868
  0.6 0.7 copy-start.5
  15.0 28.0 %all-to-all-start = ((f32[16,32,256]{2,1,0:T(8,128)}), f32[16,32,256]{2,1,0:T(8,128)S(1)}, u32[]{:S(2)}, u32[]{:S(2)}) async-start(f32[16,32,256]{2,1,0:T(8,128)} %constant_dynamic-update-slice_fusion), calls=%async_computation | async-start | bytes 1048576 | tf_op jit(solution)/shard_map/all_to_all | solution.py:113
  51.6 22.1 %all-to-all-start.1 = ((f32[16,32,256]{2,1,0:T(8,128)}), f32[16,32,256]{2,1,0:T(8,128)S(1)}, u32[]{:S(2)}, u32[]{:S(2)}) async-start(f32[16,32,256]{2,1,0:T(8,128)} %fusion.14), calls=%async_computation.1 | async-start | bytes 1048576 | tf_op jit(solution)/shard_map/all_to_all | solution.py:117
  74.1 7.7 %collective-permute-start = (f32[32,1,128]{2,1,0:T(1,128)S(1)}, f32[32,1,128]{2,1,0:T(1,128)S(1)}, u32[]{:S(2)}, u32[]{:S(2)}) collective-permute-start(f32[32,1,128]{2,1,0:T(1,128)S(1)} %get-tuple-element.41), channel_id=1, source_target_pairs={{16,0},{32,16},{48,32},{64,48},{80,64},{96,80},{112,96},{128,112},... | collective-permute-start | bytes 49160 | tf_op jit(solution)/shard_map/ppermute | solution.py:31
  78.3 4.3 %collective-permute-start.1 = (f32[32,1,128]{2,1,0:T(1,128)S(1)}, f32[32,1,128]{2,1,0:T(1,128)S(1)}, u32[]{:S(2)}, u32[]{:S(2)}) collective-permute-start(f32[32,1,128]{2,1,0:T(1,128)S(1)} %get-tuple-element.42), channel_id=1, source_target_pairs={{0,16},{16,32},{32,48},{48,64},{64,80},{80,96},{96,112},{112,128},... | collective-permute-start | bytes 49160 | tf_op jit(solution)/shard_map/ppermute | solution.py:28
  82.9 8.3 %collective-permute-start.2 = (f32[32,1,128]{2,1,0:T(1,128)S(1)}, f32[32,1,128]{2,1,0:T(1,128)S(1)}, u32[]{:S(2)}, u32[]{:S(2)}) collective-permute-start(f32[32,1,128]{2,1,0:T(1,128)S(1)} %get-tuple-element.39), channel_id=1, source_target_pairs={{16,0},{32,16},{48,32},{64,48},{80,64},{96,80},{112,96},{128,112},... | collective-permute-start | bytes 49160 | tf_op jit(solution)/shard_map/ppermute | solution.py:31
  85.6 6.4 %collective-permute-start.3 = (f32[32,1,128]{2,1,0:T(1,128)S(1)}, f32[32,1,128]{2,1,0:T(1,128)S(1)}, u32[]{:S(2)}, u32[]{:S(2)}) collective-permute-start(f32[32,1,128]{2,1,0:T(1,128)S(1)} %get-tuple-element.40), channel_id=1, source_target_pairs={{0,16},{16,32},{32,48},{48,64},{64,80},{80,96},{96,112},{112,128},... | collective-permute-start | bytes 49160 | tf_op jit(solution)/shard_map/ppermute | solution.py:28
  92.2 8.3 %collective-permute-start.4 = (f32[32,1,128]{2,1,0:T(1,128)S(1)}, f32[32,1,128]{2,1,0:T(1,128)S(1)}, u32[]{:S(2)}, u32[]{:S(2)}) collective-permute-start(f32[32,1,128]{2,1,0:T(1,128)S(1)} %get-tuple-element.37), channel_id=1, source_target_pairs={{16,0},{32,16},{48,32},{64,48},{80,64},{96,80},{112,96},{128,112},... | collective-permute-start | bytes 49160 | tf_op jit(solution)/shard_map/ppermute | solution.py:31
  94.1 7.2 %collective-permute-start.5 = (f32[32,1,128]{2,1,0:T(1,128)S(1)}, f32[32,1,128]{2,1,0:T(1,128)S(1)}, u32[]{:S(2)}, u32[]{:S(2)}) collective-permute-start(f32[32,1,128]{2,1,0:T(1,128)S(1)} %get-tuple-element.38), channel_id=1, source_target_pairs={{0,16},{16,32},{32,48},{48,64},{64,80},{80,96},{96,112},{112,128},... | collective-permute-start | bytes 49160 | tf_op jit(solution)/shard_map/ppermute | solution.py:28
  111.3 15.3 %all-to-all-start.2 = ((f32[16,32,128]{2,1,0:T(8,128)}), f32[16,32,128]{2,1,0:T(8,128)S(1)}, u32[]{:S(2)}, u32[]{:S(2)}) async-start(f32[16,32,128]{2,1,0:T(8,128)} %constant_dynamic-update-slice_fusion.16), calls=%async_computation.2 | async-start | bytes 524288 | tf_op jit(solution)/shard_map/all_to_all | solution.py:113
  197.9 7.7 %collective-permute-start.6 = (f32[32,1,128]{2,1,0:T(1,128)S(1)}, f32[32,1,128]{2,1,0:T(1,128)S(1)}, u32[]{:S(2)}, u32[]{:S(2)}) collective-permute-start(f32[32,1,128]{2,1,0:T(1,128)S(1)} %get-tuple-element.35), channel_id=1, source_target_pairs={{16,0},{32,16},{48,32},{64,48},{80,64},{96,80},{112,96},{128,112},... | collective-permute-start | bytes 49160 | tf_op jit(solution)/shard_map/ppermute | solution.py:31
  202.4 4.0 %collective-permute-start.7 = (f32[32,1,128]{2,1,0:T(1,128)S(1)}, f32[32,1,128]{2,1,0:T(1,128)S(1)}, u32[]{:S(2)}, u32[]{:S(2)}) collective-permute-start(f32[32,1,128]{2,1,0:T(1,128)S(1)} %get-tuple-element.36), channel_id=1, source_target_pairs={{0,16},{16,32},{32,48},{48,64},{64,80},{80,96},{96,112},{112,128},... | collective-permute-start | bytes 49160 | tf_op jit(solution)/shard_map/ppermute | solution.py:28
  206.7 8.3 %collective-permute-start.8 = (f32[32,1,128]{2,1,0:T(1,128)S(1)}, f32[32,1,128]{2,1,0:T(1,128)S(1)}, u32[]{:S(2)}, u32[]{:S(2)}) collective-permute-start(f32[32,1,128]{2,1,0:T(1,128)S(1)} %get-tuple-element.33), channel_id=1, source_target_pairs={{16,0},{32,16},{48,32},{64,48},{80,64},{96,80},{112,96},{128,112},... | collective-permute-start | bytes 49160 | tf_op jit(solution)/shard_map/ppermute | solution.py:31
  209.7 6.1 %collective-permute-start.9 = (f32[32,1,128]{2,1,0:T(1,128)S(1)}, f32[32,1,128]{2,1,0:T(1,128)S(1)}, u32[]{:S(2)}, u32[]{:S(2)}) collective-permute-start(f32[32,1,128]{2,1,0:T(1,128)S(1)} %get-tuple-element.34), channel_id=1, source_target_pairs={{0,16},{16,32},{32,48},{48,64},{64,80},{80,96},{96,112},{112,128},... | collective-permute-start | bytes 49160 | tf_op jit(solution)/shard_map/ppermute | solution.py:28
  216.0 8.3 %collective-permute-start.10 = (f32[32,1,128]{2,1,0:T(1,128)S(1)}, f32[32,1,128]{2,1,0:T(1,128)S(1)}, u32[]{:S(2)}, u32[]{:S(2)}) collective-permute-start(f32[32,1,128]{2,1,0:T(1,128)S(1)} %get-tuple-element.31), channel_id=1, source_target_pairs={{16,0},{32,16},{48,32},{64,48},{80,64},{96,80},{112,96},{128,112},... | collective-permute-start | bytes 49160 | tf_op jit(solution)/shard_map/ppermute | solution.py:31
  218.0 7.2 %collective-permute-start.11 = (f32[32,1,128]{2,1,0:T(1,128)S(1)}, f32[32,1,128]{2,1,0:T(1,128)S(1)}, u32[]{:S(2)}, u32[]{:S(2)}) collective-permute-start(f32[32,1,128]{2,1,0:T(1,128)S(1)} %get-tuple-element.32), channel_id=1, source_target_pairs={{0,16},{16,32},{32,48},{48,64},{64,80},{80,96},{96,112},{112,128},... | collective-permute-start | bytes 49160 | tf_op jit(solution)/shard_map/ppermute | solution.py:28
  235.2 4.3 %copy-start.7 = (s32[2,32,1]{1,2,0:T(1,128)S(1)}, s32[2,32,1]{1,2,0:T(1,128)}, u32[]{:S(2)}) copy-start(s32[2,32,1]{1,2,0:T(1,128)} %param.15) | copy-start | bytes 772
  235.2 15.4 %all-to-all-start.6 = ((f32[16,32,128]{2,1,0:T(8,128)}), f32[16,32,128]{2,1,0:T(8,128)S(1)}, u32[]{:S(2)}, u32[]{:S(2)}) async-start(f32[16,32,128]{2,1,0:T(8,128)} %constant_dynamic-update-slice_fusion.48), calls=%async_computation.6 | async-start | bytes 524288 | tf_op jit(solution)/shard_map/all_to_all | solution.py:113
  257.3 3.7 %copy-start.6 = (s32[2,32,1]{1,2,0:T(1,128)S(1)}, s32[2,32,1]{1,2,0:T(1,128)}, u32[]{:S(2)}) copy-start(s32[2,32,1]{1,2,0:T(1,128)} %param.16) | copy-start | bytes 772
  257.3 15.8 %all-to-all-start.7 = ((f32[16,32,128]{2,1,0:T(8,128)}), f32[16,32,128]{2,1,0:T(8,128)S(1)}, u32[]{:S(2)}, u32[]{:S(2)}) async-start(f32[16,32,128]{2,1,0:T(8,128)} %fusion.21), calls=%async_computation.7 | async-start | bytes 524288 | tf_op jit(solution)/shard_map/all_to_all | solution.py:117
  261.1 23.3 %collective-permute-start.12 = (f32[32,1,128]{2,0,1:T(8,128)S(1)}, f32[32,1,128]{2,0,1:T(8,128)S(1)}, u32[]{:S(2)}, u32[]{:S(2)}) collective-permute-start(f32[32,1,128]{2,0,1:T(8,128)S(1)} %get-tuple-element.30), channel_id=1, source_target_pairs={{16,0},{32,16},{48,32},{64,48},{80,64},{96,80},{112,96},{128,112},... | collective-permute-start | bytes 49160 | tf_op jit(solution)/shard_map/ppermute | solution.py:31
  263.0 20.2 %copy-start.1 = (f32[32,16,128]{2,1,0:T(8,128)S(1)}, f32[32,16,128]{2,1,0:T(8,128)}, u32[]{:S(2)}) copy-start(f32[32,16,128]{2,1,0:T(8,128)} %param.13) | copy-start | bytes 786436
  263.0 21.4 %collective-permute-start.13 = (f32[32,1,128]{2,0,1:T(8,128)S(1)}, f32[32,1,128]{2,0,1:T(8,128)S(1)}, u32[]{:S(2)}, u32[]{:S(2)}) collective-permute-start(f32[32,1,128]{2,0,1:T(8,128)S(1)} %get-tuple-element.29), channel_id=1, source_target_pairs={{0,16},{16,32},{32,48},{48,64},{64,80},{80,96},{96,112},{112,128},... | collective-permute-start | bytes 49160 | tf_op jit(solution)/shard_map/ppermute | solution.py:28
  273.2 11.2 %collective-permute-start.16 = (f32[32,1,128]{2,0,1:T(8,128)S(1)}, f32[32,1,128]{2,0,1:T(8,128)S(1)}, u32[]{:S(2)}, u32[]{:S(2)}) collective-permute-start(f32[32,1,128]{2,0,1:T(8,128)S(1)} %get-tuple-element.26), channel_id=1, source_target_pairs={{16,0},{32,16},{48,32},{64,48},{80,64},{96,80},{112,96},{128,112},... | collective-permute-start | bytes 49160 | tf_op jit(solution)/shard_map/ppermute | solution.py:31
  275.1 9.3 %collective-permute-start.17 = (f32[32,1,128]{2,0,1:T(8,128)S(1)}, f32[32,1,128]{2,0,1:T(8,128)S(1)}, u32[]{:S(2)}, u32[]{:S(2)}) collective-permute-start(f32[32,1,128]{2,0,1:T(8,128)S(1)} %get-tuple-element.25), channel_id=1, source_target_pairs={{0,16},{16,32},{32,48},{48,64},{64,80},{80,96},{96,112},{112,128},... | collective-permute-start | bytes 49160 | tf_op jit(solution)/shard_map/ppermute | solution.py:28
  285.7 16.9 %collective-permute-start.18 = (f32[32,16,128]{2,0,1:T(8,128)S(1)}, f32[32,16,128]{2,0,1:T(8,128)S(1)}, u32[]{:S(2)}, u32[]{:S(2)}) collective-permute-start(f32[32,16,128]{2,0,1:T(8,128)S(1)} %fusion.70), channel_id=1, source_target_pairs={{0,16},{16,32},{32,48},{48,64},{64,80},{80,96},{96,112},{112,128},... | collective-permute-start | bytes 786440 | tf_op jit(solution)/shard_map/ppermute | solution.py:39
  292.0 10.6 %collective-permute-start.19 = (f32[32,16,128]{2,0,1:T(8,128)S(1)}, f32[32,16,128]{2,0,1:T(8,128)S(1)}, u32[]{:S(2)}, u32[]{:S(2)}) collective-permute-start(f32[32,16,128]{2,0,1:T(8,128)S(1)} %fusion.68), channel_id=1, source_target_pairs={{16,0},{32,16},{48,32},{64,48},{80,64},{96,80},{112,96},{128,112},... | collective-permute-start | bytes 786440 | tf_op jit(solution)/shard_map/ppermute | solution.py:39
  294.3 11.5 %collective-permute-start.14 = (f32[32,16,128]{2,0,1:T(8,128)S(1)}, f32[32,16,128]{2,0,1:T(8,128)S(1)}, u32[]{:S(2)}, u32[]{:S(2)}) collective-permute-start(f32[32,16,128]{2,0,1:T(8,128)S(1)} %fusion.75), channel_id=1, source_target_pairs={{0,16},{16,32},{32,48},{48,64},{64,80},{80,96},{96,112},{112,128},... | collective-permute-start | bytes 786440 | tf_op jit(solution)/shard_map/ppermute | solution.py:39
  300.4 9.9 %collective-permute-start.15 = (f32[32,16,128]{2,0,1:T(8,128)S(1)}, f32[32,16,128]{2,0,1:T(8,128)}, u32[]{:S(2)}, u32[]{:S(2)}) collective-permute-start(f32[32,16,128]{2,0,1:T(8,128)S(1)} %fusion.73), channel_id=1, source_target_pairs={{16,0},{32,16},{48,32},{64,48},{80,64},{96,80},{112,96},{128,112},... | collective-permute-start | bytes 786440 | tf_op jit(solution)/shard_map/ppermute | solution.py:39
  314.1 1.0 copy-start.2
  314.1 1.0 copy-start.3
  314.2 1.1 copy-start.4
